TPU v7x, 512 devices: a whole 4x8x8 slice. The times are simulated.
512 devices in a mesh: dp: 8 (over y), cls: 64 (over x, z, core).
Axes of the slice: x: 4, y: 8, z: 8, core: 2. Of those that a mesh axis runs over, the one named last changes fastest.
Arguments:
- embeddings: bfloat16 [4608, 4096], P('dp'), may hold values from -128 to 128
- fold_ids: int32 [4608], P('dp'), may hold values from 0 to 4
- labels: int32 [4608], P('dp'), may hold values from 0 to 1023
- weights: bfloat16 [4096, 5120], P('dp', 'cls'), may hold values from -4 to 4
- direction: bfloat16 [4096, 5120], P('dp', 'cls'), may hold values from -0.09375 to 0.09375
Outputs:
- gradient: float32 [4096, 5120], P('dp', 'cls')
- hess_vec: float32 [4096, 5120], P('dp', 'cls')
All inputs are finite; a program needn't handle non-finite values.
Results may differ from a plain program's by a relative error of at most 0.0055.
Values may be sent and summed in bfloat16 or wider, within the bound.
No kernel may reach another device: no remote copies, remote signals or barrier semaphores. Data moves between devices by JAX's collectives and lax.ppermute only.
A program may use at most 64 MiB of HBM per device.

v0:
```python
import jax
import jax.numpy as jnp
from jax import lax
from jax.sharding import PartitionSpec as P

D = 4096
FOLDS = 5


def local(embeddings, fold_ids, labels, weights, direction):
    row_count = embeddings.shape[0]
    columns = weights.shape[1]
    per_class = columns // FOLDS
    logits = jnp.dot(
        embeddings,
        lax.all_gather(weights, "dp", axis=0, tiled=True),
        preferred_element_type=jnp.float32,
    )
    tangent = jnp.dot(
        embeddings,
        lax.all_gather(direction, "dp", axis=0, tiled=True),
        preferred_element_type=jnp.float32,
    )
    logits = logits.reshape(row_count, per_class, FOLDS)
    tangent = tangent.reshape(row_count, per_class, FOLDS)
    local_high = jnp.max(logits, axis=1)
    highest = lax.pmax(local_high, "cls")
    scaled = jnp.exp(logits - highest[:, None, :])
    summed, moment = lax.psum((jnp.sum(scaled, axis=1), jnp.sum(scaled * tangent, axis=1)), "cls")
    probability = scaled / summed[:, None, :]
    mean_tangent = moment / summed
    class_ids = lax.axis_index("cls") * per_class + jnp.arange(per_class, dtype=jnp.int32)
    onehot = (labels[:, None] == class_ids[None, :]).astype(jnp.float32)[:, :, None]
    training = (fold_ids[:, None] != jnp.arange(FOLDS, dtype=jnp.int32)[None, :]).astype(
        jnp.float32
    )[:, None, :]
    residual_rows = (
        (training * (probability - onehot)).reshape(row_count, columns).astype(jnp.bfloat16)
    )
    curvature = (
        (training * probability * (tangent - mean_tangent[:, None, :]))
        .reshape(row_count, columns)
        .astype(jnp.bfloat16)
    )
    contract = (((0,), (0,)), ((), ()))
    share = D // lax.axis_size("dp")
    full_grad, full_hvp = lax.psum(
        (
            lax.dot_general(
                embeddings, residual_rows, contract, preferred_element_type=jnp.float32
            ),
            lax.dot_general(embeddings, curvature, contract, preferred_element_type=jnp.float32),
        ),
        "dp",
    )
    offset = lax.axis_index("dp") * share
    gradient = lax.dynamic_slice_in_dim(full_grad, offset, share, 0)
    hess_vec = lax.dynamic_slice_in_dim(full_hvp, offset, share, 0)
    return (gradient, hess_vec)


def solution(mesh):
    placed = (P("dp", None), P("dp"), P("dp"), P("dp", "cls"), P("dp", "cls"))
    return jax.shard_map(
        local,
        mesh=mesh,
        in_specs=placed,
        out_specs=(P("dp", "cls"), P("dp", "cls")),
        check_vma=False,
    )
```

profile of v0, /device:TPU:6, one launch (start us, length us, event | category | flops | bytes accessed | tf_op | source)
XLA Modules:
  0.0 670.7 jit_solution(5172615857026448851)
XLA Ops:
  7.2 0.0 all-reduce.4.cloned.1.call-start
  7.2 0.7 fusion.1
  7.9 0.8 compare_convert_fusion
  8.8 0.0 copy-start
  8.8 27.7 %all_gather.6 = bf16[4096,80]{0,1:T(8,128)(2,1)S(1)} all-gather(bf16[512,80]{0,1:T(8,128)(2,1)} %param.8), channel_id=1, replica_groups=mesh['dp'=8,'cls'=64] {'dp'}, dimensions={0}, use_global_device_ids=true | all-gather | bytes 737280 | tf_op jit(solution)/shard_map/all_gather | solution.py:16
  36.5 3.9 fusion.2
  40.5 216.1 %pmax.7 = f32[576,5]{0,1:T(8,128)S(1)} all-reduce(f32[576,5]{0,1:T(8,128)S(1)} %reduce_max.9), channel_id=1, replica_groups=mesh['dp'=8,'cls'=64] {'cls'}, use_global_device_ids=true, to_apply=%region_1.0 | all-reduce | flops 2880 | bytes 23040 | tf_op jit(solution)/shard_map/pmax | solution.py:27
  256.7 0.0 copy-done
  256.7 26.0 %all_gather.7 = bf16[4096,80]{0,1:T(8,128)(2,1)S(1)} all-gather(bf16[512,80]{0,1:T(8,128)(2,1)S(1)} %copy-done), channel_id=1, replica_groups=mesh['dp'=8,'cls'=64] {'dp'}, dimensions={0}, use_global_device_ids=true | all-gather | bytes 737280 | tf_op jit(solution)/shard_map/all_gather | solution.py:21
  282.6 3.9 fusion.3
  286.6 0.1 multiply_reduce_fusion
  286.7 246.1 %all-reduce = (f32[576,5]{0,1:T(8,128)S(1)}, f32[576,5]{0,1:T(8,128)S(1)}) all-reduce(f32[576,5]{0,1:T(8,128)S(1)} %get-tuple-element.3, f32[576,5]{0,1:T(8,128)S(1)} %get-tuple-element.2), channel_id=1, replica_groups=mesh['dp'=8,'cls'=64] {'cls'}, use_global_device_ids=true, to_apply=%region_3.0 | all-reduce | flops 5760 | bytes 46080 | tf_op jit(solution)/shard_map/psum | solution.py:29
  532.9 4.5 convolution_bitcast_fusion
  537.4 4.5 convolution_bitcast_fusion.1
  541.9 0.0 all-reduce.4.cloned.1.call-update
  541.9 120.2 %all-reduce.4.cloned.1.call-done = (f32[4096,80]{0,1:T(8,128)}, f32[4096,80]{0,1:T(8,128)}) async-done(((f32[4096,80]{0,1:T(8,128)}, f32[4096,80]{0,1:T(8,128)}), (f32[4096,80]{0,1:T(8,128)}, f32[4096,80]{0,1:T(8,128)})) %all-reduce.4.cloned.1.call-update) | async-done | bytes 2621456 | tf_op jit(solution)/shard_map/psum | solution.py:47
  662.1 1.7 constant_dynamic-slice_fusion
  (15 shorter events, 0.4 us)
Async XLA Ops:
  7.2 655.0 %all-reduce.4.cloned.1.call-start = ((), (), s32[]{:S(2)}) async-start(), calls=%async_computation | async-start | bytes 5242880 | tf_op jit(solution)/shard_map/psum | solution.py:47
  8.8 247.8 %copy-start = (bf16[512,80]{0,1:T(8,128)(2,1)S(1)}, bf16[512,80]{0,1:T(8,128)(2,1)}, u32[]{:S(2)}) copy-start(bf16[512,80]{0,1:T(8,128)(2,1)} %param.9) | copy-start | bytes 245764
Sparse Core Ops, SparseCore 0:
  542.0 120.0 all-reduce.3
where the time goes:
time: 671 us
  blocking collectives  516 us (77%)
  waiting for transfers between devices  120 us (18%)
  matrix products  16.7 us (2%)
  between operations  14.2 us (2%)
    psum x1, blocking collectives, local(): lax.psum((jnp.sum(scaled, axis=1), jnp.sum(scaled * tangent, axis=1)), 'c...  246 us
    pmax x1, blocking collectives, local(): highest = lax.pmax(local_high, 'cls')  216 us
    psum x1, waiting for transfers between devices, local(): lax.psum((lax.dot_general(embeddings, residual_rows, contract, preferred_...  120 us
    all_gather x1, blocking collectives, local(): lax.all_gather(weights, 'dp', axis=0, tiled=True)  27.7 us
    all_gather x1, blocking collectives, local(): lax.all_gather(direction, 'dp', axis=0, tiled=True)  26 us
  transfers between devices with their start and end apart: 1, of which 1 were waited for; matrix products, arithmetic and copies ran while one was open for 0% of the time, Pallas kernels for 0%

commit v1 on v0

v1 whole, which is shorter than its diff:
```python
import jax
import jax.numpy as jnp
from jax import lax
from jax.sharding import PartitionSpec as P

FOLDS = 5
GATHER = "pp"


def gather_rows(x, axis, n):
    if GATHER == "ag":
        return lax.all_gather(x, axis, axis=0, tiled=True)
    me = lax.axis_index(axis)
    if GATHER == "dbl":
        held = x
        k = 0
        while (1 << k) < n:
            bit = 1 << k
            got = lax.ppermute(held, axis, [(i, i ^ bit) for i in range(n)])
            mine_low = (me & bit) == 0
            held = jnp.where(mine_low, jnp.concatenate([held, got], 0), jnp.concatenate([got, held], 0))
            k += 1
        return held
    parts = [x] + [lax.ppermute(x, axis, [(i, (i + k) % n) for i in range(n)]) for k in range(1, n)]
    reversed_parts = parts[::-1]
    doubled = jnp.concatenate(reversed_parts + reversed_parts, 0)
    start = ((n - 1 - me) % n) * x.shape[0]
    return lax.dynamic_slice_in_dim(doubled, start, n * x.shape[0], 0)


def softmax_stats(stats, axis, n):
    folds = stats.shape[1] // 3
    k = 0
    while (1 << k) < n:
        bit = 1 << k
        other = lax.ppermute(stats, axis, [(i, i ^ bit) for i in range(n)])
        m, mo = stats[:, :folds], other[:, :folds]
        top = jnp.maximum(m, mo)
        a = jnp.exp(m - top)
        b = jnp.exp(mo - top)
        a2 = jnp.concatenate([a, a], 1)
        b2 = jnp.concatenate([b, b], 1)
        rest = stats[:, folds:] * a2 + other[:, folds:] * b2
        stats = jnp.concatenate([top, rest], 1)
        k += 1
    return stats


def local(embeddings, fold_ids, labels, weights, direction):
    row_count = embeddings.shape[0]
    columns = weights.shape[1]
    per_class = columns // FOLDS
    n_dp = lax.axis_size("dp")
    n_cls = lax.axis_size("cls")
    both = gather_rows(jnp.concatenate([weights, direction], 1), "dp", n_dp)
    lt = jnp.dot(embeddings, both, preferred_element_type=jnp.float32)
    logits = lt[:, :columns].reshape(row_count, per_class, FOLDS)
    tangent = lt[:, columns:].reshape(row_count, per_class, FOLDS)
    local_high = jnp.max(logits, axis=1)
    scaled_local = jnp.exp(logits - local_high[:, None, :])
    stats = jnp.concatenate(
        [local_high, jnp.sum(scaled_local, axis=1), jnp.sum(scaled_local * tangent, axis=1)], 1
    )
    stats = softmax_stats(stats, "cls", n_cls)
    highest = stats[:, :FOLDS]
    summed = stats[:, FOLDS : 2 * FOLDS]
    moment = stats[:, 2 * FOLDS :]
    scaled = jnp.exp(logits - highest[:, None, :])
    probability = scaled / summed[:, None, :]
    mean_tangent = moment / summed
    class_ids = lax.axis_index("cls") * per_class + jnp.arange(per_class, dtype=jnp.int32)
    onehot = (labels[:, None] == class_ids[None, :]).astype(jnp.float32)[:, :, None]
    training = (fold_ids[:, None] != jnp.arange(FOLDS, dtype=jnp.int32)[None, :]).astype(
        jnp.float32
    )[:, None, :]
    residual_rows = (
        (training * (probability - onehot)).reshape(row_count, columns).astype(jnp.bfloat16)
    )
    curvature = (
        (training * probability * (tangent - mean_tangent[:, None, :]))
        .reshape(row_count, columns)
        .astype(jnp.bfloat16)
    )
    contract = (((0,), (0,)), ((), ()))
    terms = lax.dot_general(
        embeddings,
        jnp.concatenate([residual_rows, curvature], 1),
        contract,
        preferred_element_type=jnp.float32,
    )
    summed_terms = lax.psum_scatter(terms, "dp", scatter_dimension=0, tiled=True)
    return (summed_terms[:, :columns], summed_terms[:, columns:])


def solution(mesh):
    placed = (P("dp", None), P("dp"), P("dp"), P("dp", "cls"), P("dp", "cls"))
    return jax.shard_map(
        local,
        mesh=mesh,
        in_specs=placed,
        out_specs=(P("dp", "cls"), P("dp", "cls")),
        check_vma=False,
    )
```

time: 671 us -> 161 us (0.24)
  blocking collectives: 516 us -> 0 us
  starting transfers between devices: 0.04 us -> 56.6 us
  waiting for transfers between devices: 120 us -> 77.1 us
  matrix products: 16.7 us -> 6.88 us
    psum x1 -> x0, blocking collectives: 246 us -> none  [local(): lax.psum((jnp.sum(scaled, axis=1), jnp.sum(scaled * tangent, axis=1)), 'c...]
    pmax x1 -> x0, blocking collectives: 216 us -> none  [local(): highest = lax.pmax(local_high, 'cls')]
    psum x1 -> x0, waiting for transfers between devices: 120 us -> none  [local(): lax.psum((lax.dot_general(embeddings, residual_rows, contract, preferred_...]
    ppermute x0 -> x13, starting transfers between devices: none -> 56.6 us  [the longest x7 29.4 us: gather_rows(): lax.ppermute(x, axis, [(i, (i + k) % n) for i in range(n)])]
    all_gather x2 -> x0, blocking collectives: 53.7 us -> none  [the longest x1 27.7 us: local(): lax.all_gather(weights, 'dp', axis=0, tiled=True)]
    reduce_scatter x0 -> x1, waiting for transfers between devices: none -> 43.8 us  [local(): lax.psum_scatter(terms, 'dp', scatter_dimension=0, tiled=True)]
    ppermute x0 -> x13, waiting for transfers between devices: none -> 33.3 us  [the longest x7 18.5 us: gather_rows(): lax.ppermute(x, axis, [(i, (i + k) % n) for i in range(n)])]
    dot_general x4 -> x2, matrix products: 16.7 us -> 6.88 us  [the longest x1 5.05 us: local(): lax.dot_general(embeddings, jnp.concatenate([residual_rows, curvature], 1...]
  transfers between devices with their start and end apart: 1 -> 14, of which waited for: 1 -> 11; matrix products, arithmetic and copies ran while one was open for 0% -> 0% of each run, Pallas kernels for 0% -> 0%
where the time goes in v1:
time: 161 us; the launch traced here: 160 us
  waiting for transfers between devices  77.1 us (48%)
  starting transfers between devices  56.6 us (35%)
  between operations  14.7 us (9%)
  matrix products  6.88 us (4%)
  local copies, waits for them, and re-layouts  4.2 us (3%)
    reduce_scatter x1, waiting for transfers between devices, local(): lax.psum_scatter(terms, 'dp', scatter_dimension=0, tiled=True)  43.8 us
    ppermute x7, starting transfers between devices, gather_rows(): lax.ppermute(x, axis, [(i, (i + k) % n) for i in range(n)])  29.4 us
    ppermute x6, starting transfers between devices, softmax_stats(): other = lax.ppermute(stats, axis, [(i, i ^ bit) for i in range(n)])  27.2 us
    ppermute x7, waiting for transfers between devices, gather_rows(): lax.ppermute(x, axis, [(i, (i + k) % n) for i in range(n)])  18.5 us
    ppermute x6, waiting for transfers between devices, softmax_stats(): other = lax.ppermute(stats, axis, [(i, i ^ bit) for i in range(n)])  14.8 us
    dot_general x1, matrix products, local(): lax.dot_general(embeddings, jnp.concatenate([residual_rows, curvature], 1...  5.05 us
  transfers between devices with their start and end apart: 14, of which 11 were waited for; matrix products, arithmetic and copies ran while one was open for 0% of the time, Pallas kernels for 0%

profile of v1, /device:TPU:6, one launch (start us, length us, event | category | flops | bytes accessed | tf_op | source)
XLA Modules:
  0.0 160.2 jit_solution(10311879882932638402)
XLA Ops:
  7.2 0.0 copy-start.1
  7.2 0.0 copy-start.2
  7.2 0.0 reduce-scatter.2.cloned.1.call-start
  7.2 0.9 constant_dynamic-update-slice_fusion.1
  8.2 0.9 constant_dynamic-update-slice_fusion
  9.0 5.4 %collective-permute-start = (bf16[512,160]{0,1:T(8,128)(2,1)S(1)}, bf16[512,160]{0,1:T(8,128)(2,1)S(1)}, u32[]{:S(2)}, u32[]{:S(2)}) collective-permute-start(bf16[512,160]{0,1:T(8,128)(2,1)S(1)} %constant_dynamic-update-slice_fusion), channel_id=1, source_target_pairs={{0,448},{64,0},{128,64},{192,128},{256,192},{320,256},{384,320},{4... | collective-permute-start | bytes 491528 | tf_op jit(solution)/shard_map/ppermute | solution.py:24
  14.4 4.0 %collective-permute-start.1 = (bf16[512,160]{0,1:T(8,128)(2,1)S(1)}, bf16[512,160]{0,1:T(8,128)(2,1)S(1)}, u32[]{:S(2)}, u32[]{:S(2)}) collective-permute-start(bf16[512,160]{0,1:T(8,128)(2,1)S(1)} %constant_dynamic-update-slice_fusion), channel_id=1, source_target_pairs={{0,384},{64,448},{128,0},{192,64},{256,128},{320,192},{384,256},{4... | collective-permute-start | bytes 491528 | tf_op jit(solution)/shard_map/ppermute | solution.py:24
  18.5 3.0 %collective-permute-start.2 = (bf16[512,160]{0,1:T(8,128)(2,1)S(1)}, bf16[512,160]{0,1:T(8,128)(2,1)S(1)}, u32[]{:S(2)}, u32[]{:S(2)}) collective-permute-start(bf16[512,160]{0,1:T(8,128)(2,1)S(1)} %constant_dynamic-update-slice_fusion), channel_id=1, source_target_pairs={{0,320},{64,384},{128,448},{192,0},{256,64},{320,128},{384,192},{4... | collective-permute-start | bytes 491528 | tf_op jit(solution)/shard_map/ppermute | solution.py:24
  21.5 5.9 %collective-permute-start.3 = (bf16[512,160]{0,1:T(8,128)(2,1)S(1)}, bf16[512,160]{0,1:T(8,128)(2,1)S(1)}, u32[]{:S(2)}, u32[]{:S(2)}) collective-permute-start(bf16[512,160]{0,1:T(8,128)(2,1)S(1)} %constant_dynamic-update-slice_fusion), channel_id=1, source_target_pairs={{0,256},{64,320},{128,384},{192,448},{256,0},{320,64},{384,128},{4... | collective-permute-start | bytes 491528 | tf_op jit(solution)/shard_map/ppermute | solution.py:24
  27.5 1.9 %collective-permute-start.4 = (bf16[512,160]{0,1:T(8,128)(2,1)S(1)}, bf16[512,160]{0,1:T(8,128)(2,1)S(1)}, u32[]{:S(2)}, u32[]{:S(2)}) collective-permute-start(bf16[512,160]{0,1:T(8,128)(2,1)S(1)} %constant_dynamic-update-slice_fusion), channel_id=1, source_target_pairs={{0,192},{64,256},{128,320},{192,384},{256,448},{320,0},{384,64},{4... | collective-permute-start | bytes 491528 | tf_op jit(solution)/shard_map/ppermute | solution.py:24
  29.4 0.0 copy-start
  29.4 0.0 collective-permute-done
  29.4 5.6 %collective-permute-start.5 = (bf16[512,160]{0,1:T(8,128)(2,1)S(1)}, bf16[512,160]{0,1:T(8,128)(2,1)S(1)}, u32[]{:S(2)}, u32[]{:S(2)}) collective-permute-start(bf16[512,160]{0,1:T(8,128)(2,1)S(1)} %constant_dynamic-update-slice_fusion), channel_id=1, source_target_pairs={{0,128},{64,192},{128,256},{192,320},{256,384},{320,448},{384,0},{... | collective-permute-start | bytes 491528 | tf_op jit(solution)/shard_map/ppermute | solution.py:24
  35.1 0.0 collective-permute-done.1
  35.1 3.5 %collective-permute-start.6 = (bf16[512,160]{0,1:T(8,128)(2,1)S(1)}, bf16[512,160]{0,1:T(8,128)(2,1)S(1)}, u32[]{:S(2)}, u32[]{:S(2)}) collective-permute-start(bf16[512,160]{0,1:T(8,128)(2,1)S(1)} %constant_dynamic-update-slice_fusion), channel_id=1, source_target_pairs={{0,64},{64,128},{128,192},{192,256},{256,320},{320,384},{384,448},... | collective-permute-start | bytes 491528 | tf_op jit(solution)/shard_map/ppermute | solution.py:24
  38.6 0.0 collective-permute-done.2
  38.6 0.5 collective-permute-done.3
  39.1 11.5 %collective-permute-done.4 = bf16[512,160]{0,1:T(8,128)(2,1)S(1)} collective-permute-done((bf16[512,160]{0,1:T(8,128)(2,1)S(1)}, bf16[512,160]{0,1:T(8,128)(2,1)S(1)}, u32[]{:S(2)}, u32[]{:S(2)}) %collective-permute-start.4) | collective-permute-done | bytes 163872 | tf_op jit(solution)/shard_map/ppermute | solution.py:24
  50.6 3.3 %collective-permute-done.5 = bf16[512,160]{0,1:T(8,128)(2,1)S(1)} collective-permute-done((bf16[512,160]{0,1:T(8,128)(2,1)S(1)}, bf16[512,160]{0,1:T(8,128)(2,1)S(1)}, u32[]{:S(2)}, u32[]{:S(2)}) %collective-permute-start.5) | collective-permute-done | bytes 163872 | tf_op jit(solution)/shard_map/ppermute | solution.py:24
  53.9 3.3 %collective-permute-done.6 = bf16[512,160]{0,1:T(8,128)(2,1)S(1)} collective-permute-done((bf16[512,160]{0,1:T(8,128)(2,1)S(1)}, bf16[512,160]{0,1:T(8,128)(2,1)S(1)}, u32[]{:S(2)}, u32[]{:S(2)}) %collective-permute-start.6) | collective-permute-done | bytes 163872 | tf_op jit(solution)/shard_map/ppermute | solution.py:24
  57.2 0.0 copy-done.1
  57.2 0.0 copy-done.2
  57.4 0.0 copy-done
  57.4 1.8 %fusion.2 = f32[576,160]{0,1:T(8,128)S(1)} fusion(bf16[576,4096]{1,0:T(8,128)(2,1)S(1)} %copy-done, bf16[8192,160]{0,1:T(8,128)(2,1)S(1)} %constant_dynamic-update-slice_fusion.18, s32[]{:T(128)S(6)} %select_n.11), kind=kOutput, calls=%fused_computation.3 | convolution fusion | flops 754974720 | bytes 6397956 | tf_op jit(solution)/shard_map/dot_general | solution.py:56
  59.3 0.0 copy-start.3
  59.3 0.0 copy-start.4
  59.5 0.1 fusion.5
  59.6 1.9 %collective-permute-start.7 = (f32[576,15]{0,1:T(8,128)S(1)}, f32[576,15]{0,1:T(8,128)S(1)}, u32[]{:S(2)}, u32[]{:S(2)}) collective-permute-start(f32[576,15]{0,1:T(8,128)S(1)} %pad_maximum_fusion), channel_id=1, source_target_pairs={{0,1},{1,0},{2,3},{3,2},{4,5},{5,4},{6,7},{7,6},{8,9},{9,8},{10,11... | collective-permute-start | bytes 103688 | tf_op jit(solution)/shard_map/ppermute | solution.py:36
  61.5 1.2 collective-permute-done.7
  62.8 4.3 %collective-permute-start.8 = (f32[576,15]{0,1:T(8,128)S(1)}, f32[576,15]{0,1:T(8,128)S(1)}, u32[]{:S(2)}, u32[]{:S(2)}) collective-permute-start(f32[576,15]{0,1:T(8,128)S(1)} %pad_maximum_fusion.1), channel_id=1, source_target_pairs={{0,2},{1,3},{2,0},{3,1},{4,6},{5,7},{6,4},{7,5},{8,10},{9,11},{10,... | collective-permute-start | bytes 103688 | tf_op jit(solution)/shard_map/ppermute | solution.py:36
  67.1 2.0 %collective-permute-done.8 = f32[576,15]{0,1:T(8,128)S(1)} collective-permute-done((f32[576,15]{0,1:T(8,128)S(1)}, f32[576,15]{0,1:T(8,128)S(1)}, u32[]{:S(2)}, u32[]{:S(2)}) %collective-permute-start.8) | collective-permute-done | bytes 34592 | tf_op jit(solution)/shard_map/ppermute | solution.py:36
  69.1 6.1 %collective-permute-start.9 = (f32[576,15]{0,1:T(8,128)S(1)}, f32[576,15]{0,1:T(8,128)S(1)}, u32[]{:S(2)}, u32[]{:S(2)}) collective-permute-start(f32[576,15]{0,1:T(8,128)S(1)} %pad_maximum_fusion.2), channel_id=1, source_target_pairs={{0,4},{1,5},{2,6},{3,7},{4,0},{5,1},{6,2},{7,3},{8,12},{9,13},{10,... | collective-permute-start | bytes 103688 | tf_op jit(solution)/shard_map/ppermute | solution.py:36
  75.2 2.2 %collective-permute-done.9 = f32[576,15]{0,1:T(8,128)S(1)} collective-permute-done((f32[576,15]{0,1:T(8,128)S(1)}, f32[576,15]{0,1:T(8,128)S(1)}, u32[]{:S(2)}, u32[]{:S(2)}) %collective-permute-start.9) | collective-permute-done | bytes 34592 | tf_op jit(solution)/shard_map/ppermute | solution.py:36
  77.5 9.1 %collective-permute-start.10 = (f32[576,15]{0,1:T(8,128)S(1)}, f32[576,15]{0,1:T(8,128)S(1)}, u32[]{:S(2)}, u32[]{:S(2)}) collective-permute-start(f32[576,15]{0,1:T(8,128)S(1)} %pad_maximum_fusion.3), channel_id=1, source_target_pairs={{0,8},{1,9},{2,10},{3,11},{4,12},{5,13},{6,14},{7,15},{8,0},{9,1},... | collective-permute-start | bytes 103688 | tf_op jit(solution)/shard_map/ppermute | solution.py:36
  86.6 2.0 %collective-permute-done.10 = f32[576,15]{0,1:T(8,128)S(1)} collective-permute-done((f32[576,15]{0,1:T(8,128)S(1)}, f32[576,15]{0,1:T(8,128)S(1)}, u32[]{:S(2)}, u32[]{:S(2)}) %collective-permute-start.10) | collective-permute-done | bytes 34592 | tf_op jit(solution)/shard_map/ppermute | solution.py:36
  88.7 2.7 %collective-permute-start.11 = (f32[576,15]{0,1:T(8,128)S(1)}, f32[576,15]{0,1:T(8,128)S(1)}, u32[]{:S(2)}, u32[]{:S(2)}) collective-permute-start(f32[576,15]{0,1:T(8,128)S(1)} %pad_maximum_fusion.4), channel_id=1, source_target_pairs={{0,16},{1,17},{2,18},{3,19},{4,20},{5,21},{6,22},{7,23},{8,24},{9,... | collective-permute-start | bytes 103688 | tf_op jit(solution)/shard_map/ppermute | solution.py:36
  91.4 0.0 copy-done.3
  91.4 0.1 compare_convert_fusion
  91.5 3.3 %collective-permute-done.11 = f32[576,15]{0,1:T(8,128)S(1)} collective-permute-done((f32[576,15]{0,1:T(8,128)S(1)}, f32[576,15]{0,1:T(8,128)S(1)}, u32[]{:S(2)}, u32[]{:S(2)}) %collective-permute-start.11) | collective-permute-done | bytes 34592 | tf_op jit(solution)/shard_map/ppermute | solution.py:36
  94.9 3.0 %collective-permute-start.12 = (f32[576,15]{0,1:T(8,128)S(1)}, f32[576,15]{0,1:T(8,128)S(1)}, u32[]{:S(2)}, u32[]{:S(2)}) collective-permute-start(f32[576,15]{0,1:T(8,128)S(1)} %pad_maximum_fusion.5), channel_id=1, source_target_pairs={{0,32},{1,33},{2,34},{3,35},{4,36},{5,37},{6,38},{7,39},{8,40},{9,... | collective-permute-start | bytes 103688 | tf_op jit(solution)/shard_map/ppermute | solution.py:36
  98.0 0.0 copy-done.4
  98.1 4.2 %collective-permute-done.12 = f32[576,15]{0,1:T(8,128)S(1)} collective-permute-done((f32[576,15]{0,1:T(8,128)S(1)}, f32[576,15]{0,1:T(8,128)S(1)}, u32[]{:S(2)}, u32[]{:S(2)}) %collective-permute-start.12) | collective-permute-done | bytes 34592 | tf_op jit(solution)/shard_map/ppermute | solution.py:36
  102.6 0.1 multiply_convert_fusion.1
  102.7 5.1 %convolution_bitcast_fusion = f32[4096,160]{0,1:T(8,128)} fusion(bf16[576,4096]{1,0:T(8,128)(2,1)} %param.5, bf16[576,80]{0,1:T(8,128)(2,1)S(1)} %get-tuple-element.17, bf16[576,80]{0,1:T(8,128)(2,1)S(1)} %get-tuple-element.16), kind=kOutput, calls=%fused_computation | convolution fusion | flops 755343360 | bytes 7524352 | tf_op jit(solution)/shard_map/dot_general | solution.py:85
  107.8 0.0 reduce-scatter.2.cloned.1.call-update
  107.8 43.8 %reduce-scatter.2.cloned.1.call-done = f32[512,160]{0,1:T(8,128)} async-done(((f32[4096,160]{0,1:T(8,128)}), f32[512,160]{0,1:T(8,128)}) %reduce-scatter.2.cloned.1.call-update) | async-done | bytes 327696 | tf_op jit(solution)/shard_map/reduce_scatter | solution.py:91
  151.6 1.7 %fusion.19 = (f32[512,80]{0,1:T(8,128)}, f32[512,80]{0,1:T(8,128)}) fusion(f32[512,160]{0,1:T(8,128)} %reduce-scatter.2.cloned.1.call-done), kind=kLoop, calls=%fused_computation.83 | loop fusion | bytes 655360 | tf_op jit(solution)/shard_map/slice | solution.py:92
  (59 shorter events, 1.0 us)
Async XLA Ops:
  7.2 50.0 %copy-start.1 = (bf16[512,80]{0,1:T(8,128)(2,1)S(1)}, bf16[512,80]{0,1:T(8,128)(2,1)}, u32[]{:S(2)}) copy-start(bf16[512,80]{0,1:T(8,128)(2,1)} %param.8) | copy-start | bytes 245764
  7.2 50.1 %copy-start.2 = (bf16[512,80]{0,1:T(8,128)(2,1)S(1)}, bf16[512,80]{0,1:T(8,128)(2,1)}, u32[]{:S(2)}) copy-start(bf16[512,80]{0,1:T(8,128)(2,1)} %param.9) | copy-start | bytes 245764
  7.2 144.4 %reduce-scatter.2.cloned.1.call-start = ((), (), s32[]{:S(2)}) async-start(), calls=%async_computation.1 | async-start | bytes 2949120 | tf_op jit(solution)/shard_map/reduce_scatter | solution.py:91
  9.0 20.4 %collective-permute-start = (bf16[512,160]{0,1:T(8,128)(2,1)S(1)}, bf16[512,160]{0,1:T(8,128)(2,1)S(1)}, u32[]{:S(2)}, u32[]{:S(2)}) collective-permute-start(bf16[512,160]{0,1:T(8,128)(2,1)S(1)} %constant_dynamic-update-slice_fusion), channel_id=1, source_target_pairs={{0,448},{64,0},{128,64},{192,128},{256,192},{320,256},{384,320},{4... | collective-permute-start | bytes 491528 | tf_op jit(solution)/shard_map/ppermute | solution.py:24
  14.4 20.7 %collective-permute-start.1 = (bf16[512,160]{0,1:T(8,128)(2,1)S(1)}, bf16[512,160]{0,1:T(8,128)(2,1)S(1)}, u32[]{:S(2)}, u32[]{:S(2)}) collective-permute-start(bf16[512,160]{0,1:T(8,128)(2,1)S(1)} %constant_dynamic-update-slice_fusion), channel_id=1, source_target_pairs={{0,384},{64,448},{128,0},{192,64},{256,128},{320,192},{384,256},{4... | collective-permute-start | bytes 491528 | tf_op jit(solution)/shard_map/ppermute | solution.py:24
  18.5 20.1 %collective-permute-start.2 = (bf16[512,160]{0,1:T(8,128)(2,1)S(1)}, bf16[512,160]{0,1:T(8,128)(2,1)S(1)}, u32[]{:S(2)}, u32[]{:S(2)}) collective-permute-start(bf16[512,160]{0,1:T(8,128)(2,1)S(1)} %constant_dynamic-update-slice_fusion), channel_id=1, source_target_pairs={{0,320},{64,384},{128,448},{192,0},{256,64},{320,128},{384,192},{4... | collective-permute-start | bytes 491528 | tf_op jit(solution)/shard_map/ppermute | solution.py:24
  21.5 17.6 %collective-permute-start.3 = (bf16[512,160]{0,1:T(8,128)(2,1)S(1)}, bf16[512,160]{0,1:T(8,128)(2,1)S(1)}, u32[]{:S(2)}, u32[]{:S(2)}) collective-permute-start(bf16[512,160]{0,1:T(8,128)(2,1)S(1)} %constant_dynamic-update-slice_fusion), channel_id=1, source_target_pairs={{0,256},{64,320},{128,384},{192,448},{256,0},{320,64},{384,128},{4... | collective-permute-start | bytes 491528 | tf_op jit(solution)/shard_map/ppermute | solution.py:24
  27.5 23.1 %collective-permute-start.4 = (bf16[512,160]{0,1:T(8,128)(2,1)S(1)}, bf16[512,160]{0,1:T(8,128)(2,1)S(1)}, u32[]{:S(2)}, u32[]{:S(2)}) collective-permute-start(bf16[512,160]{0,1:T(8,128)(2,1)S(1)} %constant_dynamic-update-slice_fusion), channel_id=1, source_target_pairs={{0,192},{64,256},{128,320},{192,384},{256,448},{320,0},{384,64},{4... | collective-permute-start | bytes 491528 | tf_op jit(solution)/shard_map/ppermute | solution.py:24
  29.4 28.0 %copy-start = (bf16[576,4096]{1,0:T(8,128)(2,1)S(1)}, bf16[576,4096]{1,0:T(8,128)(2,1)}, u32[]{:S(2)}) copy-start(bf16[576,4096]{1,0:T(8,128)(2,1)} %param.5) | copy-start | bytes 14155780
  29.4 24.5 %collective-permute-start.5 = (bf16[512,160]{0,1:T(8,128)(2,1)S(1)}, bf16[512,160]{0,1:T(8,128)(2,1)S(1)}, u32[]{:S(2)}, u32[]{:S(2)}) collective-permute-start(bf16[512,160]{0,1:T(8,128)(2,1)S(1)} %constant_dynamic-update-slice_fusion), channel_id=1, source_target_pairs={{0,128},{64,192},{128,256},{192,320},{256,384},{320,448},{384,0},{... | collective-permute-start | bytes 491528 | tf_op jit(solution)/shard_map/ppermute | solution.py:24
  35.1 22.1 %collective-permute-start.6 = (bf16[512,160]{0,1:T(8,128)(2,1)S(1)}, bf16[512,160]{0,1:T(8,128)(2,1)S(1)}, u32[]{:S(2)}, u32[]{:S(2)}) collective-permute-start(bf16[512,160]{0,1:T(8,128)(2,1)S(1)} %constant_dynamic-update-slice_fusion), channel_id=1, source_target_pairs={{0,64},{64,128},{128,192},{192,256},{256,320},{320,384},{384,448},... | collective-permute-start | bytes 491528 | tf_op jit(solution)/shard_map/ppermute | solution.py:24
  59.3 32.1 %copy-start.3 = (s32[576]{0:T(1024)S(1)}, s32[576]{0:T(1024)}, u32[]{:S(2)}) copy-start(s32[576]{0:T(1024)} %param.7) | copy-start | bytes 6916
  59.3 38.7 %copy-start.4 = (s32[576]{0:T(1024)S(1)}, s32[576]{0:T(1024)}, u32[]{:S(2)}) copy-start(s32[576]{0:T(1024)} %param.6) | copy-start | bytes 6916
  59.6 3.1 %collective-permute-start.7 = (f32[576,15]{0,1:T(8,128)S(1)}, f32[576,15]{0,1:T(8,128)S(1)}, u32[]{:S(2)}, u32[]{:S(2)}) collective-permute-start(f32[576,15]{0,1:T(8,128)S(1)} %pad_maximum_fusion), channel_id=1, source_target_pairs={{0,1},{1,0},{2,3},{3,2},{4,5},{5,4},{6,7},{7,6},{8,9},{9,8},{10,11... | collective-permute-start | bytes 103688 | tf_op jit(solution)/shard_map/ppermute | solution.py:36
  62.8 6.2 %collective-permute-start.8 = (f32[576,15]{0,1:T(8,128)S(1)}, f32[576,15]{0,1:T(8,128)S(1)}, u32[]{:S(2)}, u32[]{:S(2)}) collective-permute-start(f32[576,15]{0,1:T(8,128)S(1)} %pad_maximum_fusion.1), channel_id=1, source_target_pairs={{0,2},{1,3},{2,0},{3,1},{4,6},{5,7},{6,4},{7,5},{8,10},{9,11},{10,... | collective-permute-start | bytes 103688 | tf_op jit(solution)/shard_map/ppermute | solution.py:36
  69.1 8.3 %collective-permute-start.9 = (f32[576,15]{0,1:T(8,128)S(1)}, f32[576,15]{0,1:T(8,128)S(1)}, u32[]{:S(2)}, u32[]{:S(2)}) collective-permute-start(f32[576,15]{0,1:T(8,128)S(1)} %pad_maximum_fusion.2), channel_id=1, source_target_pairs={{0,4},{1,5},{2,6},{3,7},{4,0},{5,1},{6,2},{7,3},{8,12},{9,13},{10,... | collective-permute-start | bytes 103688 | tf_op jit(solution)/shard_map/ppermute | solution.py:36
  77.5 11.1 %collective-permute-start.10 = (f32[576,15]{0,1:T(8,128)S(1)}, f32[576,15]{0,1:T(8,128)S(1)}, u32[]{:S(2)}, u32[]{:S(2)}) collective-permute-start(f32[576,15]{0,1:T(8,128)S(1)} %pad_maximum_fusion.3), channel_id=1, source_target_pairs={{0,8},{1,9},{2,10},{3,11},{4,12},{5,13},{6,14},{7,15},{8,0},{9,1},... | collective-permute-start | bytes 103688 | tf_op jit(solution)/shard_map/ppermute | solution.py:36
  88.7 6.2 %collective-permute-start.11 = (f32[576,15]{0,1:T(8,128)S(1)}, f32[576,15]{0,1:T(8,128)S(1)}, u32[]{:S(2)}, u32[]{:S(2)}) collective-permute-start(f32[576,15]{0,1:T(8,128)S(1)} %pad_maximum_fusion.4), channel_id=1, source_target_pairs={{0,16},{1,17},{2,18},{3,19},{4,20},{5,21},{6,22},{7,23},{8,24},{9,... | collective-permute-start | bytes 103688 | tf_op jit(solution)/shard_map/ppermute | solution.py:36
  94.9 7.4 %collective-permute-start.12 = (f32[576,15]{0,1:T(8,128)S(1)}, f32[576,15]{0,1:T(8,128)S(1)}, u32[]{:S(2)}, u32[]{:S(2)}) collective-permute-start(f32[576,15]{0,1:T(8,128)S(1)} %pad_maximum_fusion.5), channel_id=1, source_target_pairs={{0,32},{1,33},{2,34},{3,35},{4,36},{5,37},{6,38},{7,39},{8,40},{9,... | collective-permute-start | bytes 103688 | tf_op jit(solution)/shard_map/ppermute | solution.py:36
Sparse Core Ops, SparseCore 0:
  107.9 43.6 reduce-scatter.1

commit v2 on v1

--- a/solution.py
+++ b/solution.py
@@ -1,10 +1,12 @@
 import jax
 import jax.numpy as jnp
 from jax import lax
-from jax.sharding import PartitionSpec as P
+from jax.sharding import Mesh, PartitionSpec as P
 
 FOLDS = 5
-GATHER = "pp"
+CLS = ("x", "z", "c")
+GATHER = "ag"
+STATS = "ag2"
 
 
 def gather_rows(x, axis, n):
@@ -46,12 +48,22 @@
     return stats
 
 
+def combine_many(gathered):
+    folds = gathered.shape[2] // 3
+    m = gathered[:, :, :folds]
+    top = jnp.max(m, axis=0)
+    scale = jnp.exp(m - top[None])
+    summed = jnp.sum(gathered[:, :, folds : 2 * folds] * scale, axis=0)
+    moment = jnp.sum(gathered[:, :, 2 * folds :] * scale, axis=0)
+    return jnp.concatenate([top, summed, moment], 1)
+
+
 def local(embeddings, fold_ids, labels, weights, direction):
     row_count = embeddings.shape[0]
     columns = weights.shape[1]
     per_class = columns // FOLDS
     n_dp = lax.axis_size("dp")
-    n_cls = lax.axis_size("cls")
+    n_cls = lax.axis_size(CLS)
     both = gather_rows(jnp.concatenate([weights, direction], 1), "dp", n_dp)
     lt = jnp.dot(embeddings, both, preferred_element_type=jnp.float32)
     logits = lt[:, :columns].reshape(row_count, per_class, FOLDS)
@@ -61,14 +73,18 @@
     stats = jnp.concatenate(
         [local_high, jnp.sum(scaled_local, axis=1), jnp.sum(scaled_local * tangent, axis=1)], 1
     )
-    stats = softmax_stats(stats, "cls", n_cls)
+    if STATS == "ag2":
+        stats = combine_many(lax.all_gather(stats, ("z", "c"), axis=0, tiled=False))
+        stats = combine_many(lax.all_gather(stats, "x", axis=0, tiled=False))
+    else:
+        stats = softmax_stats(stats, CLS, n_cls)
     highest = stats[:, :FOLDS]
     summed = stats[:, FOLDS : 2 * FOLDS]
     moment = stats[:, 2 * FOLDS :]
     scaled = jnp.exp(logits - highest[:, None, :])
     probability = scaled / summed[:, None, :]
     mean_tangent = moment / summed
-    class_ids = lax.axis_index("cls") * per_class + jnp.arange(per_class, dtype=jnp.int32)
+    class_ids = lax.axis_index(CLS) * per_class + jnp.arange(per_class, dtype=jnp.int32)
     onehot = (labels[:, None] == class_ids[None, :]).astype(jnp.float32)[:, :, None]
     training = (fold_ids[:, None] != jnp.arange(FOLDS, dtype=jnp.int32)[None, :]).astype(
         jnp.float32
@@ -92,12 +108,20 @@
     return (summed_terms[:, :columns], summed_terms[:, columns:])
 
 
+def split_mesh(mesh):
+    row = mesh.devices[0]
+    nx = len({d.coords[0] for d in row})
+    nz = len({d.coords[2] for d in row})
+    nc = len(row) // (nx * nz)
+    return Mesh(mesh.devices.reshape(mesh.devices.shape[0], nx, nz, nc), ("dp",) + CLS)
+
+
 def solution(mesh):
-    placed = (P("dp", None), P("dp"), P("dp"), P("dp", "cls"), P("dp", "cls"))
+    placed = (P("dp", None), P("dp"), P("dp"), P("dp", CLS), P("dp", CLS))
     return jax.shard_map(
         local,
-        mesh=mesh,
+        mesh=split_mesh(mesh),
         in_specs=placed,
-        out_specs=(P("dp", "cls"), P("dp", "cls")),
+        out_specs=(P("dp", CLS), P("dp", CLS)),
         check_vma=False,
     )

time: 161 us -> 150 us (0.932)
  starting transfers between devices: 56.6 us -> 0.08 us
  blocking collectives: 0 us -> 32.1 us
  waiting for transfers between devices: 77.1 us -> 88.4 us
  other arithmetic: 0.7 us -> 3.59 us
  matrix products: 6.88 us -> 9.6 us
  local copies, waits for them, and re-layouts: 4.2 us -> 2.14 us
    ppermute x13 -> x0, starting transfers between devices: 56.6 us -> none  [the longest x7 29.4 us: gather_rows(): lax.ppermute(x, axis, [(i, (i + k) % n) for i in range(n)])]
    all_gather x0 -> x1, waiting for transfers between devices: none -> 46.5 us  [gather_rows(): return lax.all_gather(x, axis, axis=0, tiled=True)]
    ppermute x13 -> x0, waiting for transfers between devices: 33.3 us -> none  [the longest x7 18.5 us: gather_rows(): lax.ppermute(x, axis, [(i, (i + k) % n) for i in range(n)])]
    all_gather x0 -> x2, blocking collectives: none -> 32.1 us  [the longest x1 19.9 us: local(): stats = combine_many(lax.all_gather(stats, ('z', 'c'), axis=0, tiled=False))]
    dot_general x1, matrix products: 1.83 us -> 4.54 us  [local(): lt = jnp.dot(embeddings, both, preferred_element_type=jnp.float32)]
    reduce_scatter x1, waiting for transfers between devices: 43.8 us -> 41.9 us  [local(): lax.psum_scatter(terms, 'dp', scatter_dimension=0, tiled=True)]
  transfers between devices with their start and end apart: 14 -> 2, of which waited for: 11 -> 2; matrix products, arithmetic and copies ran while one was open for 0% -> 1% of each run, Pallas kernels for 0% -> 0%
where the time goes in v2:
time: 150 us
  waiting for transfers between devices  88.4 us (59%)
  blocking collectives  32.1 us (21%)
  between operations  14.2 us (9%)
  matrix products  9.6 us (6%)
  other arithmetic  3.59 us (2%)
  local copies, waits for them, and re-layouts  2.14 us (1%)
    all_gather x1, waiting for transfers between devices, gather_rows(): return lax.all_gather(x, axis, axis=0, tiled=True)  46.5 us
    reduce_scatter x1, waiting for transfers between devices, local(): lax.psum_scatter(terms, 'dp', scatter_dimension=0, tiled=True)  41.9 us
    all_gather x1, blocking collectives, local(): stats = combine_many(lax.all_gather(stats, ('z', 'c'), axis=0, tiled=False))  19.9 us
    all_gather x1, blocking collectives, local(): stats = combine_many(lax.all_gather(stats, 'x', axis=0, tiled=False))  12.2 us
    dot_general x1, matrix products, local(): lax.dot_general(embeddings, jnp.concatenate([residual_rows, curvature], 1...  5.06 us
    dot_general x1, matrix products, local(): lt = jnp.dot(embeddings, both, preferred_element_type=jnp.float32)  4.54 us
  transfers between devices with their start and end apart: 2, of which 2 were waited for; matrix products, arithmetic and copies ran while one was open for 1% of the time, Pallas kernels for 0%

profile of v2, /device:TPU:6, one launch (start us, length us, event | category | flops | bytes accessed | tf_op | source)
XLA Modules:
  0.0 150.1 jit_solution(2581435711192839990)
XLA Ops:
  7.2 0.0 all-gather.6.cloned.1.call-start
  7.2 1.6 %pad_maximum_fusion = bf16[512,160]{0,1:T(8,128)(2,1)} fusion(bf16[512,80]{0,1:T(8,128)(2,1)} %param.9, bf16[512,80]{0,1:T(8,128)(2,1)} %param.8), kind=kLoop, calls=%fused_computation.17 | loop fusion | flops 327680 | bytes 327680 | tf_op jit(solution)/shard_map/concatenate | solution.py:67
  8.8 0.0 all-gather.6.cloned.1.call-update
  8.8 0.0 reduce-scatter.2.cloned.1.call-start
  8.9 0.8 compare_convert_fusion
  9.7 0.7 fusion.8
  10.5 46.5 %all-gather.6.cloned.1.call-done = bf16[4096,160]{0,1:T(8,128)(2,1)} async-done(((bf16[512,160]{0,1:T(8,128)(2,1)}), bf16[4096,160]{0,1:T(8,128)(2,1)}) %all-gather.6.cloned.1.call-update) | async-done | bytes 1310736 | tf_op jit(solution)/shard_map/all_gather | solution.py:14
  57.0 4.5 %convolution_bitcast_fusion.1 = f32[576,160]{0,1:T(8,128)S(1)} fusion(bf16[4096,160]{0,1:T(8,128)(2,1)} %all-gather.6.cloned.1.call-done, bf16[576,4096]{1,0:T(8,128)(2,1)} %param.5), kind=kOutput, calls=%fused_computation.1 | convolution fusion | flops 754974720 | bytes 6397952 | tf_op jit(solution)/shard_map/dot_general | solution.py:68
  61.8 0.1 fusion.2
  61.9 19.9 %all-gather.2 = f32[16,576,15]{1,2,0:T(8,128)S(1)} all-gather(f32[1,576,15]{1,2,0:T(8,128)S(1)} %maximum_bitcast_fusion), channel_id=2, replica_groups=mesh['dp'=8,'x'=4,'z'=8,'c'=2] {'z','c'}, dimensions={0}, use_global_device_ids=true | all-gather | bytes 587520 | tf_op jit(solution)/shard_map/all_gather | solution.py:77
  81.8 0.1 fusion.1
  82.0 12.2 %all-gather.3 = f32[4,576,15]{1,2,0:T(8,128)S(1)} all-gather(f32[1,576,15]{1,2,0:T(8,128)S(1)} %maximum_bitcast_fusion.1), channel_id=3, replica_groups=mesh['dp'=8,'x'=4,'z'=8,'c'=2] {'x'}, dimensions={0}, use_global_device_ids=true | all-gather | bytes 172800 | tf_op jit(solution)/shard_map/all_gather | solution.py:78
  94.5 0.1 multiply_convert_fusion.1
  94.6 5.1 %convolution_bitcast_fusion = f32[4096,160]{0,1:T(8,128)} fusion(bf16[576,4096]{1,0:T(8,128)(2,1)} %param.5, bf16[576,80]{0,1:T(8,128)(2,1)S(1)} %get-tuple-element.9, bf16[576,80]{0,1:T(8,128)(2,1)S(1)} %get-tuple-element.8), kind=kOutput, calls=%fused_computation | convolution fusion | flops 755343360 | bytes 7524352 | tf_op jit(solution)/shard_map/dot_general | solution.py:101
  99.6 0.0 reduce-scatter.2.cloned.1.call-update
  99.7 41.9 %reduce-scatter.2.cloned.1.call-done = f32[512,160]{0,1:T(8,128)} async-done(((f32[4096,160]{0,1:T(8,128)}), f32[512,160]{0,1:T(8,128)}) %reduce-scatter.2.cloned.1.call-update) | async-done | bytes 327696 | tf_op jit(solution)/shard_map/reduce_scatter | solution.py:107
  141.5 1.7 %fusion.11 = (f32[512,80]{0,1:T(8,128)}, f32[512,80]{0,1:T(8,128)}) fusion(f32[512,160]{0,1:T(8,128)} %reduce-scatter.2.cloned.1.call-done), kind=kLoop, calls=%fused_computation.32 | loop fusion | bytes 655360 | tf_op jit(solution)/shard_map/slice | solution.py:108
  (21 shorter events, 0.6 us)
Async XLA Ops:
  7.2 49.9 %all-gather.6.cloned.1.call-start = ((), (), s32[]{:S(2)}) async-start(), calls=%async_computation.1 | async-start | bytes 1474560 | tf_op jit(solution)/shard_map/all_gather | solution.py:14
  8.8 132.7 %reduce-scatter.2.cloned.1.call-start = ((), (), s32[]{:S(2)}) async-start(), calls=%async_computation.2 | async-start | bytes 2949120 | tf_op jit(solution)/shard_map/reduce_scatter | solution.py:107
Sparse Core Ops, SparseCore 0:
  10.7 46.3 all-gather.5
  99.8 41.6 reduce-scatter.1

commit v3 on v2

--- a/solution.py
+++ b/solution.py
@@ -64,8 +64,15 @@
     per_class = columns // FOLDS
     n_dp = lax.axis_size("dp")
     n_cls = lax.axis_size(CLS)
-    both = gather_rows(jnp.concatenate([weights, direction], 1), "dp", n_dp)
-    lt = jnp.dot(embeddings, both, preferred_element_type=jnp.float32)
+    mine = jnp.concatenate([weights, direction], 1)
+    share = mine.shape[0]
+    me = lax.axis_index("dp")
+    lt = None
+    for k in range(n_dp):
+        part = mine if k == 0 else lax.ppermute(mine, "dp", [(i, (i + k) % n_dp) for i in range(n_dp)])
+        cols = lax.dynamic_slice_in_dim(embeddings, ((me - k) % n_dp) * share, share, 1)
+        step = jnp.dot(cols, part, preferred_element_type=jnp.float32)
+        lt = step if lt is None else lt + step
     logits = lt[:, :columns].reshape(row_count, per_class, FOLDS)
     tangent = lt[:, columns:].reshape(row_count, per_class, FOLDS)
     local_high = jnp.max(logits, axis=1)

time: 150 us -> 144 us (0.960)
  waiting for transfers between devices: 88.4 us -> 44.3 us
  starting transfers between devices: 0.08 us -> 29.2 us
  blocking collectives: 32.1 us -> 37.2 us
  matrix products: 9.6 us -> 12.4 us
  local copies, waits for them, and re-layouts: 2.14 us -> 3.94 us
  other arithmetic: 3.59 us -> 1.98 us
    all_gather x1 -> x0, waiting for transfers between devices: 46.5 us -> none  [gather_rows(): return lax.all_gather(x, axis, axis=0, tiled=True)]
    ppermute x0 -> x7, starting transfers between devices: none -> 29.2 us  [local(): lax.ppermute(mine, 'dp', [(i, (i + k) % n_dp) for i in range(n_dp)])]
    all_gather x1, blocking collectives: 19.9 us -> 25 us  [local(): stats = combine_many(lax.all_gather(stats, ('z', 'c'), axis=0, tiled=False))]
    ppermute x0 -> x7, waiting for transfers between devices: none -> 2.89 us  [local(): lax.ppermute(mine, 'dp', [(i, (i + k) % n_dp) for i in range(n_dp)])]
    dot_general x1 -> x8, matrix products: 4.54 us -> 7.37 us  [local(): step = jnp.dot(cols, part, preferred_element_type=jnp.float32)]
    concatenate x1 -> x0, other arithmetic: 1.6 us -> none  [local(): both = gather_rows(jnp.concatenate([weights, direction], 1), 'dp', n_dp)]
  transfers between devices with their start and end apart: 2 -> 8, of which waited for: 2 -> 2; matrix products, arithmetic and copies ran while one was open for 1% -> 6% of each run, Pallas kernels for 0% -> 0%
where the time goes in v3:
time: 144 us
  waiting for transfers between devices  44.3 us (31%)
  blocking collectives  37.2 us (26%)
  starting transfers between devices  29.2 us (20%)
  between operations  14.6 us (10%)
  matrix products  12.4 us (9%)
  local copies, waits for them, and re-layouts  3.94 us (3%)
  other arithmetic  1.98 us (1%)
    reduce_scatter x1, waiting for transfers between devices, local(): lax.psum_scatter(terms, 'dp', scatter_dimension=0, tiled=True)  41.4 us
    ppermute x7, starting transfers between devices, local(): lax.ppermute(mine, 'dp', [(i, (i + k) % n_dp) for i in range(n_dp)])  29.2 us
    all_gather x1, blocking collectives, local(): stats = combine_many(lax.all_gather(stats, ('z', 'c'), axis=0, tiled=False))  25 us
    all_gather x1, blocking collectives, local(): stats = combine_many(lax.all_gather(stats, 'x', axis=0, tiled=False))  12.2 us
    dot_general x8, matrix products, local(): step = jnp.dot(cols, part, preferred_element_type=jnp.float32)  7.37 us
    dot_general x1, matrix products, local(): lax.dot_general(embeddings, jnp.concatenate([residual_rows, curvature], 1...  5.04 us
    ppermute x7, waiting for transfers between devices, local(): lax.ppermute(mine, 'dp', [(i, (i + k) % n_dp) for i in range(n_dp)])  2.89 us
  transfers between devices with their start and end apart: 8, of which 2 were waited for; matrix products, arithmetic and copies ran while one was open for 6% of the time, Pallas kernels for 0%

profile of v3, /device:TPU:6, one launch (start us, length us, event | category | flops | bytes accessed | tf_op | source)
XLA Modules:
  0.0 143.6 jit_solution(5804788447492652084)
XLA Ops:
  7.2 0.0 reduce-scatter.2.cloned.1.call-start
  7.2 0.9 constant_dynamic-update-slice_fusion.1
  8.1 0.9 constant_dynamic-update-slice_fusion
  9.0 3.5 %collective-permute-start = (bf16[512,160]{0,1:T(8,128)(2,1)S(1)}, bf16[512,160]{0,1:T(8,128)(2,1)S(1)}, u32[]{:S(2)}, u32[]{:S(2)}) collective-permute-start(bf16[512,160]{0,1:T(8,128)(2,1)S(1)} %constant_dynamic-update-slice_fusion), channel_id=1, source_target_pairs={{0,64},{64,128},{128,192},{192,256},{256,320},{320,384},{384,448},... | collective-permute-start | bytes 491528 | tf_op jit(solution)/shard_map/ppermute | solution.py:72
  12.5 6.8 %collective-permute-start.3 = (bf16[512,160]{0,1:T(8,128)(2,1)S(1)}, bf16[512,160]{0,1:T(8,128)(2,1)S(1)}, u32[]{:S(2)}, u32[]{:S(2)}) collective-permute-start(bf16[512,160]{0,1:T(8,128)(2,1)S(1)} %constant_dynamic-update-slice_fusion), channel_id=1, source_target_pairs={{0,256},{64,320},{128,384},{192,448},{256,0},{320,64},{384,128},{4... | collective-permute-start | bytes 491528 | tf_op jit(solution)/shard_map/ppermute | solution.py:72
  19.3 2.1 %collective-permute-start.2 = (bf16[512,160]{0,1:T(8,128)(2,1)S(1)}, bf16[512,160]{0,1:T(8,128)(2,1)S(1)}, u32[]{:S(2)}, u32[]{:S(2)}) collective-permute-start(bf16[512,160]{0,1:T(8,128)(2,1)S(1)} %constant_dynamic-update-slice_fusion), channel_id=1, source_target_pairs={{0,192},{64,256},{128,320},{192,384},{256,448},{320,0},{384,64},{4... | collective-permute-start | bytes 491528 | tf_op jit(solution)/shard_map/ppermute | solution.py:72
  21.5 5.1 %collective-permute-start.6 = (bf16[512,160]{0,1:T(8,128)(2,1)S(1)}, bf16[512,160]{0,1:T(8,128)(2,1)S(1)}, u32[]{:S(2)}, u32[]{:S(2)}) collective-permute-start(bf16[512,160]{0,1:T(8,128)(2,1)S(1)} %constant_dynamic-update-slice_fusion), channel_id=1, source_target_pairs={{0,448},{64,0},{128,64},{192,128},{256,192},{320,256},{384,320},{4... | collective-permute-start | bytes 491528 | tf_op jit(solution)/shard_map/ppermute | solution.py:72
  26.6 4.0 %collective-permute-start.5 = (bf16[512,160]{0,1:T(8,128)(2,1)S(1)}, bf16[512,160]{0,1:T(8,128)(2,1)S(1)}, u32[]{:S(2)}, u32[]{:S(2)}) collective-permute-start(bf16[512,160]{0,1:T(8,128)(2,1)S(1)} %constant_dynamic-update-slice_fusion), channel_id=1, source_target_pairs={{0,384},{64,448},{128,0},{192,64},{256,128},{320,192},{384,256},{4... | collective-permute-start | bytes 491528 | tf_op jit(solution)/shard_map/ppermute | solution.py:72
  30.8 0.8 compare_convert_fusion
  31.7 0.7 fusion.27
  32.5 0.0 copy-start
  32.5 1.6 %fusion.17 = f32[576,160]{0,1:T(8,128)S(1)} fusion(bf16[512,160]{0,1:T(8,128)(2,1)S(1)} %constant_dynamic-update-slice_fusion, bf16[576,4096]{1,0:T(8,128)(2,1)} %param.5, s32[]{:T(128)S(6)} %select_n.60), kind=kOutput, calls=%fused_computation.20 | convolution fusion | flops 94371840 | bytes 1122308 | tf_op jit(solution)/shard_map/dot_general | solution.py:74
  34.1 0.0 collective-permute-done
  34.1 3.0 %collective-permute-start.4 = (bf16[512,160]{0,1:T(8,128)(2,1)S(1)}, bf16[512,160]{0,1:T(8,128)(2,1)S(1)}, u32[]{:S(2)}, u32[]{:S(2)}) collective-permute-start(bf16[512,160]{0,1:T(8,128)(2,1)S(1)} %constant_dynamic-update-slice_fusion), channel_id=1, source_target_pairs={{0,320},{64,384},{128,448},{192,0},{256,64},{320,128},{384,192},{4... | collective-permute-start | bytes 491528 | tf_op jit(solution)/shard_map/ppermute | solution.py:72
  37.1 1.4 convolution_add_fusion.1
  38.6 0.0 collective-permute-done.3
  38.6 4.5 %collective-permute-start.1 = (bf16[512,160]{0,1:T(8,128)(2,1)S(1)}, bf16[512,160]{0,1:T(8,128)(2,1)S(1)}, u32[]{:S(2)}, u32[]{:S(2)}) collective-permute-start(bf16[512,160]{0,1:T(8,128)(2,1)S(1)} %constant_dynamic-update-slice_fusion), channel_id=1, source_target_pairs={{0,128},{64,192},{128,256},{192,320},{256,384},{320,448},{384,0},{... | collective-permute-start | bytes 491528 | tf_op jit(solution)/shard_map/ppermute | solution.py:72
  43.1 1.4 fusion.11
  44.5 0.0 collective-permute-done.2
  44.5 1.4 fusion.13
  46.0 0.0 collective-permute-done.6
  46.0 0.0 copy-done
  46.0 0.4 fusion.5
  46.4 0.0 collective-permute-done.5
  46.4 0.4 fusion.7
  46.8 2.9 %collective-permute-done.4 = bf16[512,160]{0,1:T(8,128)(2,1)S(1)} collective-permute-done((bf16[512,160]{0,1:T(8,128)(2,1)S(1)}, bf16[512,160]{0,1:T(8,128)(2,1)S(1)}, u32[]{:S(2)}, u32[]{:S(2)}) %collective-permute-start.4) | collective-permute-done | bytes 163872 | tf_op jit(solution)/shard_map/ppermute | solution.py:72
  49.6 0.4 fusion.9
  50.0 0.0 collective-permute-done.1
  50.0 0.4 fusion.4
  50.6 0.1 fusion.21
  50.7 25.0 %all-gather.2 = f32[16,576,15]{1,2,0:T(8,128)S(1)} all-gather(f32[1,576,15]{1,2,0:T(8,128)S(1)} %maximum_bitcast_fusion), channel_id=2, replica_groups=mesh['dp'=8,'x'=4,'z'=8,'c'=2] {'z','c'}, dimensions={0}, use_global_device_ids=true | all-gather | bytes 587520 | tf_op jit(solution)/shard_map/all_gather | solution.py:84
  75.7 0.1 fusion.20
  75.9 12.2 %all-gather.3 = f32[4,576,15]{1,2,0:T(8,128)S(1)} all-gather(f32[1,576,15]{1,2,0:T(8,128)S(1)} %maximum_bitcast_fusion.1), channel_id=3, replica_groups=mesh['dp'=8,'x'=4,'z'=8,'c'=2] {'x'}, dimensions={0}, use_global_device_ids=true | all-gather | bytes 172800 | tf_op jit(solution)/shard_map/all_gather | solution.py:85
  88.4 0.1 multiply_convert_fusion.1
  88.5 5.0 %convolution_bitcast_fusion = f32[4096,160]{0,1:T(8,128)} fusion(bf16[576,4096]{1,0:T(8,128)(2,1)} %param.5, bf16[576,80]{0,1:T(8,128)(2,1)S(1)} %get-tuple-element.9, bf16[576,80]{0,1:T(8,128)(2,1)S(1)} %get-tuple-element.8), kind=kOutput, calls=%fused_computation | convolution fusion | flops 755343360 | bytes 7524352 | tf_op jit(solution)/shard_map/dot_general | solution.py:108
  93.5 0.0 reduce-scatter.2.cloned.1.call-update
  93.6 41.4 %reduce-scatter.2.cloned.1.call-done = f32[512,160]{0,1:T(8,128)} async-done(((f32[4096,160]{0,1:T(8,128)}), f32[512,160]{0,1:T(8,128)}) %reduce-scatter.2.cloned.1.call-update) | async-done | bytes 327696 | tf_op jit(solution)/shard_map/reduce_scatter | solution.py:114
  135.0 1.7 %fusion.38 = (f32[512,80]{0,1:T(8,128)}, f32[512,80]{0,1:T(8,128)}) fusion(f32[512,160]{0,1:T(8,128)} %reduce-scatter.2.cloned.1.call-done), kind=kLoop, calls=%fused_computation.61 | loop fusion | bytes 655360 | tf_op jit(solution)/shard_map/slice | solution.py:115
  (21 shorter events, 0.6 us)
Async XLA Ops:
  7.2 127.8 %reduce-scatter.2.cloned.1.call-start = ((), (), s32[]{:S(2)}) async-start(), calls=%async_computation.1 | async-start | bytes 2949120 | tf_op jit(solution)/shard_map/reduce_scatter | solution.py:114
  9.0 25.1 %collective-permute-start = (bf16[512,160]{0,1:T(8,128)(2,1)S(1)}, bf16[512,160]{0,1:T(8,128)(2,1)S(1)}, u32[]{:S(2)}, u32[]{:S(2)}) collective-permute-start(bf16[512,160]{0,1:T(8,128)(2,1)S(1)} %constant_dynamic-update-slice_fusion), channel_id=1, source_target_pairs={{0,64},{64,128},{128,192},{192,256},{256,320},{320,384},{384,448},... | collective-permute-start | bytes 491528 | tf_op jit(solution)/shard_map/ppermute | solution.py:72
  12.5 26.1 %collective-permute-start.3 = (bf16[512,160]{0,1:T(8,128)(2,1)S(1)}, bf16[512,160]{0,1:T(8,128)(2,1)S(1)}, u32[]{:S(2)}, u32[]{:S(2)}) collective-permute-start(bf16[512,160]{0,1:T(8,128)(2,1)S(1)} %constant_dynamic-update-slice_fusion), channel_id=1, source_target_pairs={{0,256},{64,320},{128,384},{192,448},{256,0},{320,64},{384,128},{4... | collective-permute-start | bytes 491528 | tf_op jit(solution)/shard_map/ppermute | solution.py:72
  19.3 25.2 %collective-permute-start.2 = (bf16[512,160]{0,1:T(8,128)(2,1)S(1)}, bf16[512,160]{0,1:T(8,128)(2,1)S(1)}, u32[]{:S(2)}, u32[]{:S(2)}) collective-permute-start(bf16[512,160]{0,1:T(8,128)(2,1)S(1)} %constant_dynamic-update-slice_fusion), channel_id=1, source_target_pairs={{0,192},{64,256},{128,320},{192,384},{256,448},{320,0},{384,64},{4... | collective-permute-start | bytes 491528 | tf_op jit(solution)/shard_map/ppermute | solution.py:72
  21.5 24.5 %collective-permute-start.6 = (bf16[512,160]{0,1:T(8,128)(2,1)S(1)}, bf16[512,160]{0,1:T(8,128)(2,1)S(1)}, u32[]{:S(2)}, u32[]{:S(2)}) collective-permute-start(bf16[512,160]{0,1:T(8,128)(2,1)S(1)} %constant_dynamic-update-slice_fusion), channel_id=1, source_target_pairs={{0,448},{64,0},{128,64},{192,128},{256,192},{320,256},{384,320},{4... | collective-permute-start | bytes 491528 | tf_op jit(solution)/shard_map/ppermute | solution.py:72
  26.6 19.7 %collective-permute-start.5 = (bf16[512,160]{0,1:T(8,128)(2,1)S(1)}, bf16[512,160]{0,1:T(8,128)(2,1)S(1)}, u32[]{:S(2)}, u32[]{:S(2)}) collective-permute-start(bf16[512,160]{0,1:T(8,128)(2,1)S(1)} %constant_dynamic-update-slice_fusion), channel_id=1, source_target_pairs={{0,384},{64,448},{128,0},{192,64},{256,128},{320,192},{384,256},{4... | collective-permute-start | bytes 491528 | tf_op jit(solution)/shard_map/ppermute | solution.py:72
  32.5 13.5 %copy-start = (bf16[576,4096]{1,0:T(8,128)(2,1)S(1)}, bf16[576,4096]{1,0:T(8,128)(2,1)}, u32[]{:S(2)}) copy-start(bf16[576,4096]{1,0:T(8,128)(2,1)} %param.5) | copy-start | bytes 14155780
  34.1 15.5 %collective-permute-start.4 = (bf16[512,160]{0,1:T(8,128)(2,1)S(1)}, bf16[512,160]{0,1:T(8,128)(2,1)S(1)}, u32[]{:S(2)}, u32[]{:S(2)}) collective-permute-start(bf16[512,160]{0,1:T(8,128)(2,1)S(1)} %constant_dynamic-update-slice_fusion), channel_id=1, source_target_pairs={{0,320},{64,384},{128,448},{192,0},{256,64},{320,128},{384,192},{4... | collective-permute-start | bytes 491528 | tf_op jit(solution)/shard_map/ppermute | solution.py:72
  38.6 11.4 %collective-permute-start.1 = (bf16[512,160]{0,1:T(8,128)(2,1)S(1)}, bf16[512,160]{0,1:T(8,128)(2,1)S(1)}, u32[]{:S(2)}, u32[]{:S(2)}) collective-permute-start(bf16[512,160]{0,1:T(8,128)(2,1)S(1)} %constant_dynamic-update-slice_fusion), channel_id=1, source_target_pairs={{0,128},{64,192},{128,256},{192,320},{256,384},{320,448},{384,0},{... | collective-permute-start | bytes 491528 | tf_op jit(solution)/shard_map/ppermute | solution.py:72
Sparse Core Ops, SparseCore 0:
  93.7 41.2 reduce-scatter.1

commit v4 on v3

--- a/solution.py
+++ b/solution.py
@@ -105,13 +105,16 @@
         .astype(jnp.bfloat16)
     )
     contract = (((0,), (0,)), ((), ()))
-    terms = lax.dot_general(
-        embeddings,
-        jnp.concatenate([residual_rows, curvature], 1),
-        contract,
-        preferred_element_type=jnp.float32,
-    )
-    summed_terms = lax.psum_scatter(terms, "dp", scatter_dimension=0, tiled=True)
+    both_terms = jnp.concatenate([residual_rows, curvature], 1)
+    feature_share = embeddings.shape[1] // n_dp
+    summed_terms = None
+    for k in range(n_dp):
+        rows = lax.dynamic_slice_in_dim(embeddings, ((me + k) % n_dp) * feature_share, feature_share, 1)
+        block = lax.dot_general(rows, both_terms, contract, preferred_element_type=jnp.float32)
+        if k:
+            sent = lax.ppermute(block.astype(jnp.bfloat16), "dp", [(i, (i + k) % n_dp) for i in range(n_dp)])
+            block = sent.astype(jnp.float32)
+        summed_terms = block if summed_terms is None else summed_terms + block
     return (summed_terms[:, :columns], summed_terms[:, columns:])
 
 

time: 144 us -> 141 us (0.979)
  starting transfers between devices: 29.2 us -> 59.8 us
  waiting for transfers between devices: 44.3 us -> 17.9 us
  between operations: 14.6 us -> 1.44 us
  matrix products: 12.4 us -> 18.4 us
    reduce_scatter x1 -> x0, waiting for transfers between devices: 41.4 us -> none  [local(): lax.psum_scatter(terms, 'dp', scatter_dimension=0, tiled=True)]
    ppermute x0 -> x7, starting transfers between devices: none -> 29.5 us  [local(): lax.ppermute(block.astype(jnp.bfloat16), 'dp', [(i, (i + k) % n_dp) for i...]
    ppermute x0 -> x7, waiting for transfers between devices: none -> 11.1 us  [local(): lax.ppermute(block.astype(jnp.bfloat16), 'dp', [(i, (i + k) % n_dp) for i...]
    dot_general x1 -> x8, matrix products: 5.04 us -> 11 us  [local(): lax.dot_general(rows, both_terms, contract, preferred_element_type=jnp.fl...]
    ppermute x7, waiting for transfers between devices: 2.89 us -> 6.84 us  [local(): lax.ppermute(mine, 'dp', [(i, (i + k) % n_dp) for i in range(n_dp)])]
  transfers between devices with their start and end apart: 8 -> 14, of which waited for: 2 -> 5; matrix products, arithmetic and copies ran while one was open for 6% -> 12% of each run, Pallas kernels for 0% -> 0%
where the time goes in v4:
time: 141 us; the launch traced here: 140 us
  starting transfers between devices  59.8 us (42%)
  blocking collectives  37.2 us (26%)
  matrix products  18.4 us (13%)
  waiting for transfers between devices  17.9 us (13%)
  local copies, waits for them, and re-layouts  2.94 us (2%)
  other arithmetic  1.97 us (1%)
  between operations  1.44 us (1%)
    ppermute x7, starting transfers between devices, local(): lax.ppermute(mine, 'dp', [(i, (i + k) % n_dp) for i in range(n_dp)])  30.4 us
    ppermute x7, starting transfers between devices, local(): lax.ppermute(block.astype(jnp.bfloat16), 'dp', [(i, (i + k) % n_dp) for i...  29.5 us
    all_gather x1, blocking collectives, local(): stats = combine_many(lax.all_gather(stats, ('z', 'c'), axis=0, tiled=False))  24.9 us
    all_gather x1, blocking collectives, local(): stats = combine_many(lax.all_gather(stats, 'x', axis=0, tiled=False))  12.2 us
    ppermute x7, waiting for transfers between devices, local(): lax.ppermute(block.astype(jnp.bfloat16), 'dp', [(i, (i + k) % n_dp) for i...  11.1 us
    dot_general x8, matrix products, local(): lax.dot_general(rows, both_terms, contract, preferred_element_type=jnp.fl...  11 us
    dot_general x8, matrix products, local(): step = jnp.dot(cols, part, preferred_element_type=jnp.float32)  7.36 us
    ppermute x7, waiting for transfers between devices, local(): lax.ppermute(mine, 'dp', [(i, (i + k) % n_dp) for i in range(n_dp)])  6.84 us
  transfers between devices with their start and end apart: 14, of which 5 were waited for; matrix products, arithmetic and copies ran while one was open for 12% of the time, Pallas kernels for 0%

profile of v4, /device:TPU:6, one launch (start us, length us, event | category | flops | bytes accessed | tf_op | source)
XLA Modules:
  0.0 139.6 jit_solution(9985203492260430508)
XLA Ops:
  0.6 0.9 constant_dynamic-update-slice_fusion.1
  1.5 0.9 constant_dynamic-update-slice_fusion
  2.4 3.5 %collective-permute-start = (bf16[512,160]{0,1:T(8,128)(2,1)S(1)}, bf16[512,160]{0,1:T(8,128)(2,1)S(1)}, u32[]{:S(2)}, u32[]{:S(2)}) collective-permute-start(bf16[512,160]{0,1:T(8,128)(2,1)S(1)} %constant_dynamic-update-slice_fusion), channel_id=1, source_target_pairs={{0,64},{64,128},{128,192},{192,256},{256,320},{320,384},{384,448},... | collective-permute-start | bytes 491528 | tf_op jit(solution)/shard_map/ppermute | solution.py:72
  5.9 3.8 %collective-permute-start.6 = (bf16[512,160]{0,1:T(8,128)(2,1)S(1)}, bf16[512,160]{0,1:T(8,128)(2,1)S(1)}, u32[]{:S(2)}, u32[]{:S(2)}) collective-permute-start(bf16[512,160]{0,1:T(8,128)(2,1)S(1)} %constant_dynamic-update-slice_fusion), channel_id=1, source_target_pairs={{0,448},{64,0},{128,64},{192,128},{256,192},{320,256},{384,320},{4... | collective-permute-start | bytes 491528 | tf_op jit(solution)/shard_map/ppermute | solution.py:72
  9.7 4.7 %collective-permute-start.5 = (bf16[512,160]{0,1:T(8,128)(2,1)S(1)}, bf16[512,160]{0,1:T(8,128)(2,1)S(1)}, u32[]{:S(2)}, u32[]{:S(2)}) collective-permute-start(bf16[512,160]{0,1:T(8,128)(2,1)S(1)} %constant_dynamic-update-slice_fusion), channel_id=1, source_target_pairs={{0,384},{64,448},{128,0},{192,64},{256,128},{320,192},{384,256},{4... | collective-permute-start | bytes 491528 | tf_op jit(solution)/shard_map/ppermute | solution.py:72
  14.4 4.7 %collective-permute-start.4 = (bf16[512,160]{0,1:T(8,128)(2,1)S(1)}, bf16[512,160]{0,1:T(8,128)(2,1)S(1)}, u32[]{:S(2)}, u32[]{:S(2)}) collective-permute-start(bf16[512,160]{0,1:T(8,128)(2,1)S(1)} %constant_dynamic-update-slice_fusion), channel_id=1, source_target_pairs={{0,320},{64,384},{128,448},{192,0},{256,64},{320,128},{384,192},{4... | collective-permute-start | bytes 491528 | tf_op jit(solution)/shard_map/ppermute | solution.py:72
  19.1 4.3 %collective-permute-start.3 = (bf16[512,160]{0,1:T(8,128)(2,1)S(1)}, bf16[512,160]{0,1:T(8,128)(2,1)S(1)}, u32[]{:S(2)}, u32[]{:S(2)}) collective-permute-start(bf16[512,160]{0,1:T(8,128)(2,1)S(1)} %constant_dynamic-update-slice_fusion), channel_id=1, source_target_pairs={{0,256},{64,320},{128,384},{192,448},{256,0},{320,64},{384,128},{4... | collective-permute-start | bytes 491528 | tf_op jit(solution)/shard_map/ppermute | solution.py:72
  23.7 0.8 compare_convert_fusion
  24.5 0.7 fusion.33
  25.4 0.0 copy-start
  25.4 1.6 %fusion.26 = f32[576,160]{0,1:T(8,128)S(1)} fusion(bf16[512,160]{0,1:T(8,128)(2,1)S(1)} %constant_dynamic-update-slice_fusion, bf16[576,4096]{1,0:T(8,128)(2,1)} %param.5, s32[]{:T(128)S(6)} %select_n.112), kind=kOutput, calls=%fused_computation.35 | convolution fusion | flops 94371840 | bytes 1122308 | tf_op jit(solution)/shard_map/dot_general | solution.py:74
  27.0 0.0 collective-permute-done
  27.0 3.4 %collective-permute-start.2 = (bf16[512,160]{0,1:T(8,128)(2,1)S(1)}, bf16[512,160]{0,1:T(8,128)(2,1)S(1)}, u32[]{:S(2)}, u32[]{:S(2)}) collective-permute-start(bf16[512,160]{0,1:T(8,128)(2,1)S(1)} %constant_dynamic-update-slice_fusion), channel_id=1, source_target_pairs={{0,192},{64,256},{128,320},{192,384},{256,448},{320,0},{384,64},{4... | collective-permute-start | bytes 491528 | tf_op jit(solution)/shard_map/ppermute | solution.py:72
  30.4 1.4 %convolution_add_fusion.1 = f32[576,160]{0,1:T(8,128)S(1)} fusion(f32[576,160]{0,1:T(8,128)S(1)} %fusion.26, bf16[512,160]{0,1:T(8,128)(2,1)S(1)} %collective-permute-done, bf16[576,4096]{1,0:T(8,128)(2,1)} %param.5, s32[]{:T(128)S(6)} %select_n.114), kind=kOutput, calls=%fused_computation.1 | convolution fusion | flops 94464000 | bytes 1490948 | tf_op jit(solution)/shard_map/dot_general | solution.py:74
  31.8 0.0 collective-permute-done.6
  31.8 6.0 %collective-permute-start.1 = (bf16[512,160]{0,1:T(8,128)(2,1)S(1)}, bf16[512,160]{0,1:T(8,128)(2,1)S(1)}, u32[]{:S(2)}, u32[]{:S(2)}) collective-permute-start(bf16[512,160]{0,1:T(8,128)(2,1)S(1)} %constant_dynamic-update-slice_fusion), channel_id=1, source_target_pairs={{0,128},{64,192},{128,256},{192,320},{256,384},{320,448},{384,0},{... | collective-permute-start | bytes 491528 | tf_op jit(solution)/shard_map/ppermute | solution.py:72
  37.8 1.4 %fusion.12 = f32[576,160]{0,1:T(8,128)S(1)} fusion(bf16[512,160]{0,1:T(8,128)(2,1)S(1)} %collective-permute-done.6, bf16[576,4096]{1,0:T(8,128)(2,1)} %param.5, s32[]{:T(128)S(6)} %select_n.126), kind=kOutput, calls=%fused_computation.21 | convolution fusion | flops 94371840 | bytes 1122308 | tf_op jit(solution)/shard_map/dot_general | solution.py:74
  39.3 0.0 collective-permute-done.5
  39.3 1.4 %fusion.14 = f32[576,160]{0,1:T(8,128)S(1)} fusion(bf16[512,160]{0,1:T(8,128)(2,1)S(1)} %collective-permute-done.5, bf16[576,4096]{1,0:T(8,128)(2,1)} %param.5, s32[]{:T(128)S(6)} %select_n.124), kind=kOutput, calls=%fused_computation.23 | convolution fusion | flops 94371840 | bytes 1122308 | tf_op jit(solution)/shard_map/dot_general | solution.py:74
  40.7 0.0 collective-permute-done.4
  40.7 0.0 copy-done
  40.7 0.4 fusion.16
  41.1 0.0 collective-permute-done.3
  41.1 0.4 fusion.18
  41.5 3.9 %collective-permute-done.2 = bf16[512,160]{0,1:T(8,128)(2,1)S(1)} collective-permute-done((bf16[512,160]{0,1:T(8,128)(2,1)S(1)}, bf16[512,160]{0,1:T(8,128)(2,1)S(1)}, u32[]{:S(2)}, u32[]{:S(2)}) %collective-permute-start.2) | collective-permute-done | bytes 163872 | tf_op jit(solution)/shard_map/ppermute | solution.py:72
  45.4 0.4 fusion.20
  45.8 3.0 %collective-permute-done.1 = bf16[512,160]{0,1:T(8,128)(2,1)S(1)} collective-permute-done((bf16[512,160]{0,1:T(8,128)(2,1)S(1)}, bf16[512,160]{0,1:T(8,128)(2,1)S(1)}, u32[]{:S(2)}, u32[]{:S(2)}) %collective-permute-start.1) | collective-permute-done | bytes 163872 | tf_op jit(solution)/shard_map/ppermute | solution.py:72
  48.7 0.4 fusion.4
  49.3 0.1 fusion.30
  49.4 24.9 %all-gather.2 = f32[16,576,15]{1,2,0:T(8,128)S(1)} all-gather(f32[1,576,15]{1,2,0:T(8,128)S(1)} %maximum_bitcast_fusion), channel_id=2, replica_groups=mesh['dp'=8,'x'=4,'z'=8,'c'=2] {'z','c'}, dimensions={0}, use_global_device_ids=true | all-gather | bytes 587520 | tf_op jit(solution)/shard_map/all_gather | solution.py:84
  74.4 0.1 fusion.29
  74.5 12.2 %all-gather.3 = f32[4,576,15]{1,2,0:T(8,128)S(1)} all-gather(f32[1,576,15]{1,2,0:T(8,128)S(1)} %maximum_bitcast_fusion.1), channel_id=3, replica_groups=mesh['dp'=8,'x'=4,'z'=8,'c'=2] {'x'}, dimensions={0}, use_global_device_ids=true | all-gather | bytes 172800 | tf_op jit(solution)/shard_map/all_gather | solution.py:85
  87.1 0.1 multiply_convert_fusion.1
  87.2 1.4 convolution_convert_fusion.6
  88.5 5.4 %collective-permute-start.7 = (bf16[512,160]{0,1:T(8,128)(2,1)S(1)}, bf16[512,160]{0,1:T(8,128)(2,1)S(1)}, u32[]{:S(2)}, u32[]{:S(2)}) collective-permute-start(bf16[512,160]{0,1:T(8,128)(2,1)S(1)} %convolution_convert_fusion.6), channel_id=1, source_target_pairs={{0,64},{64,128},{128,192},{192,256},{256,320},{320,384},{384,448},... | collective-permute-start | bytes 491528 | tf_op jit(solution)/shard_map/ppermute | solution.py:115
  94.0 1.4 convolution_convert_fusion.5
  95.3 1.9 %collective-permute-start.8 = (bf16[512,160]{0,1:T(8,128)(2,1)S(1)}, bf16[512,160]{0,1:T(8,128)(2,1)S(1)}, u32[]{:S(2)}, u32[]{:S(2)}) collective-permute-start(bf16[512,160]{0,1:T(8,128)(2,1)S(1)} %convolution_convert_fusion.5), channel_id=1, source_target_pairs={{0,128},{64,192},{128,256},{192,320},{256,384},{320,448},{384,0},{... | collective-permute-start | bytes 491528 | tf_op jit(solution)/shard_map/ppermute | solution.py:115
  97.3 1.4 convolution_convert_fusion.4
  98.6 4.0 %collective-permute-start.9 = (bf16[512,160]{0,1:T(8,128)(2,1)S(1)}, bf16[512,160]{0,1:T(8,128)(2,1)S(1)}, u32[]{:S(2)}, u32[]{:S(2)}) collective-permute-start(bf16[512,160]{0,1:T(8,128)(2,1)S(1)} %convolution_convert_fusion.4), channel_id=1, source_target_pairs={{0,192},{64,256},{128,320},{192,384},{256,448},{320,0},{384,64},{4... | collective-permute-start | bytes 491528 | tf_op jit(solution)/shard_map/ppermute | solution.py:115
  102.6 1.4 convolution_convert_fusion.3
  104.0 5.8 %collective-permute-start.10 = (bf16[512,160]{0,1:T(8,128)(2,1)S(1)}, bf16[512,160]{0,1:T(8,128)(2,1)S(1)}, u32[]{:S(2)}, u32[]{:S(2)}) collective-permute-start(bf16[512,160]{0,1:T(8,128)(2,1)S(1)} %convolution_convert_fusion.3), channel_id=1, source_target_pairs={{0,256},{64,320},{128,384},{192,448},{256,0},{320,64},{384,128},{4... | collective-permute-start | bytes 491528 | tf_op jit(solution)/shard_map/ppermute | solution.py:115
  109.8 1.4 convolution_convert_fusion.2
  111.1 4.3 %collective-permute-start.11 = (bf16[512,160]{0,1:T(8,128)(2,1)S(1)}, bf16[512,160]{0,1:T(8,128)(2,1)S(1)}, u32[]{:S(2)}, u32[]{:S(2)}) collective-permute-start(bf16[512,160]{0,1:T(8,128)(2,1)S(1)} %convolution_convert_fusion.2), channel_id=1, source_target_pairs={{0,320},{64,384},{128,448},{192,0},{256,64},{320,128},{384,192},{4... | collective-permute-start | bytes 491528 | tf_op jit(solution)/shard_map/ppermute | solution.py:115
  115.5 1.4 convolution_convert_fusion.1
  116.8 1.4 convolution_convert_fusion
  118.2 0.0 collective-permute-done.7
  118.2 4.8 %collective-permute-start.12 = (bf16[512,160]{0,1:T(8,128)(2,1)S(1)}, bf16[512,160]{0,1:T(8,128)(2,1)S(1)}, u32[]{:S(2)}, u32[]{:S(2)}) collective-permute-start(bf16[512,160]{0,1:T(8,128)(2,1)S(1)} %convolution_convert_fusion.1), channel_id=1, source_target_pairs={{0,384},{64,448},{128,0},{192,64},{256,128},{320,192},{384,256},{4... | collective-permute-start | bytes 491528 | tf_op jit(solution)/shard_map/ppermute | solution.py:115
  123.0 0.0 collective-permute-done.8
  123.0 3.3 %collective-permute-start.13 = (bf16[512,160]{0,1:T(8,128)(2,1)S(1)}, bf16[512,160]{0,1:T(8,128)(2,1)S(1)}, u32[]{:S(2)}, u32[]{:S(2)}) collective-permute-start(bf16[512,160]{0,1:T(8,128)(2,1)S(1)} %convolution_convert_fusion), channel_id=1, source_target_pairs={{0,448},{64,0},{128,64},{192,128},{256,192},{320,256},{384,320},{4... | collective-permute-start | bytes 491528 | tf_op jit(solution)/shard_map/ppermute | solution.py:115
  126.3 0.0 collective-permute-done.9
  126.3 0.0 collective-permute-done.10
  126.3 2.6 %collective-permute-done.11 = bf16[512,160]{0,1:T(8,128)(2,1)S(1)} collective-permute-done((bf16[512,160]{0,1:T(8,128)(2,1)S(1)}, bf16[512,160]{0,1:T(8,128)(2,1)S(1)}, u32[]{:S(2)}, u32[]{:S(2)}) %collective-permute-start.11) | collective-permute-done | bytes 163872 | tf_op jit(solution)/shard_map/ppermute | solution.py:115
  128.9 6.6 %collective-permute-done.12 = bf16[512,160]{0,1:T(8,128)(2,1)S(1)} collective-permute-done((bf16[512,160]{0,1:T(8,128)(2,1)S(1)}, bf16[512,160]{0,1:T(8,128)(2,1)S(1)}, u32[]{:S(2)}, u32[]{:S(2)}) %collective-permute-start.12) | collective-permute-done | bytes 163872 | tf_op jit(solution)/shard_map/ppermute | solution.py:115
  135.6 1.8 %collective-permute-done.13 = bf16[512,160]{0,1:T(8,128)(2,1)S(1)} collective-permute-done((bf16[512,160]{0,1:T(8,128)(2,1)S(1)}, bf16[512,160]{0,1:T(8,128)(2,1)S(1)}, u32[]{:S(2)}, u32[]{:S(2)}) %collective-permute-start.13) | collective-permute-done | bytes 163872 | tf_op jit(solution)/shard_map/ppermute | solution.py:115
  137.4 1.5 %convert_add_fusion = f32[512,160]{0,1:T(8,128)S(1)} fusion(bf16[512,160]{0,1:T(8,128)(2,1)S(1)} %collective-permute-done.13, bf16[512,160]{0,1:T(8,128)(2,1)S(1)} %collective-permute-done.12, bf16[512,160]{0,1:T(8,128)(2,1)S(1)} %collective-permute-done.11, bf16[512,160]{0,1:T(8,128)(2,1)S(1)} %collective-permute-done.10, ...), kind=kOutput, calls=%fused_computation.41 | convolution fusion | flops 95887360 | bytes 2248708 | tf_op jit(solution)/shard_map/dot_general | solution.py:113
  138.8 0.7 fusion.53
  (21 shorter events, 0.6 us)
Async XLA Ops:
  2.4 24.5 %collective-permute-start = (bf16[512,160]{0,1:T(8,128)(2,1)S(1)}, bf16[512,160]{0,1:T(8,128)(2,1)S(1)}, u32[]{:S(2)}, u32[]{:S(2)}) collective-permute-start(bf16[512,160]{0,1:T(8,128)(2,1)S(1)} %constant_dynamic-update-slice_fusion), channel_id=1, source_target_pairs={{0,64},{64,128},{128,192},{192,256},{256,320},{320,384},{384,448},... | collective-permute-start | bytes 491528 | tf_op jit(solution)/shard_map/ppermute | solution.py:72
  5.9 25.9 %collective-permute-start.6 = (bf16[512,160]{0,1:T(8,128)(2,1)S(1)}, bf16[512,160]{0,1:T(8,128)(2,1)S(1)}, u32[]{:S(2)}, u32[]{:S(2)}) collective-permute-start(bf16[512,160]{0,1:T(8,128)(2,1)S(1)} %constant_dynamic-update-slice_fusion), channel_id=1, source_target_pairs={{0,448},{64,0},{128,64},{192,128},{256,192},{320,256},{384,320},{4... | collective-permute-start | bytes 491528 | tf_op jit(solution)/shard_map/ppermute | solution.py:72
  9.7 29.6 %collective-permute-start.5 = (bf16[512,160]{0,1:T(8,128)(2,1)S(1)}, bf16[512,160]{0,1:T(8,128)(2,1)S(1)}, u32[]{:S(2)}, u32[]{:S(2)}) collective-permute-start(bf16[512,160]{0,1:T(8,128)(2,1)S(1)} %constant_dynamic-update-slice_fusion), channel_id=1, source_target_pairs={{0,384},{64,448},{128,0},{192,64},{256,128},{320,192},{384,256},{4... | collective-permute-start | bytes 491528 | tf_op jit(solution)/shard_map/ppermute | solution.py:72
  14.4 26.3 %collective-permute-start.4 = (bf16[512,160]{0,1:T(8,128)(2,1)S(1)}, bf16[512,160]{0,1:T(8,128)(2,1)S(1)}, u32[]{:S(2)}, u32[]{:S(2)}) collective-permute-start(bf16[512,160]{0,1:T(8,128)(2,1)S(1)} %constant_dynamic-update-slice_fusion), channel_id=1, source_target_pairs={{0,320},{64,384},{128,448},{192,0},{256,64},{320,128},{384,192},{4... | collective-permute-start | bytes 491528 | tf_op jit(solution)/shard_map/ppermute | solution.py:72
  19.1 22.0 %collective-permute-start.3 = (bf16[512,160]{0,1:T(8,128)(2,1)S(1)}, bf16[512,160]{0,1:T(8,128)(2,1)S(1)}, u32[]{:S(2)}, u32[]{:S(2)}) collective-permute-start(bf16[512,160]{0,1:T(8,128)(2,1)S(1)} %constant_dynamic-update-slice_fusion), channel_id=1, source_target_pairs={{0,256},{64,320},{128,384},{192,448},{256,0},{320,64},{384,128},{4... | collective-permute-start | bytes 491528 | tf_op jit(solution)/shard_map/ppermute | solution.py:72
  25.4 15.4 %copy-start = (bf16[576,4096]{1,0:T(8,128)(2,1)S(1)}, bf16[576,4096]{1,0:T(8,128)(2,1)}, u32[]{:S(2)}) copy-start(bf16[576,4096]{1,0:T(8,128)(2,1)} %param.5) | copy-start | bytes 14155780
  27.0 18.4 %collective-permute-start.2 = (bf16[512,160]{0,1:T(8,128)(2,1)S(1)}, bf16[512,160]{0,1:T(8,128)(2,1)S(1)}, u32[]{:S(2)}, u32[]{:S(2)}) collective-permute-start(bf16[512,160]{0,1:T(8,128)(2,1)S(1)} %constant_dynamic-update-slice_fusion), channel_id=1, source_target_pairs={{0,192},{64,256},{128,320},{192,384},{256,448},{320,0},{384,64},{4... | collective-permute-start | bytes 491528 | tf_op jit(solution)/shard_map/ppermute | solution.py:72
  31.8 16.9 %collective-permute-start.1 = (bf16[512,160]{0,1:T(8,128)(2,1)S(1)}, bf16[512,160]{0,1:T(8,128)(2,1)S(1)}, u32[]{:S(2)}, u32[]{:S(2)}) collective-permute-start(bf16[512,160]{0,1:T(8,128)(2,1)S(1)} %constant_dynamic-update-slice_fusion), channel_id=1, source_target_pairs={{0,128},{64,192},{128,256},{192,320},{256,384},{320,448},{384,0},{... | collective-permute-start | bytes 491528 | tf_op jit(solution)/shard_map/ppermute | solution.py:72
  88.5 29.7 %collective-permute-start.7 = (bf16[512,160]{0,1:T(8,128)(2,1)S(1)}, bf16[512,160]{0,1:T(8,128)(2,1)S(1)}, u32[]{:S(2)}, u32[]{:S(2)}) collective-permute-start(bf16[512,160]{0,1:T(8,128)(2,1)S(1)} %convolution_convert_fusion.6), channel_id=1, source_target_pairs={{0,64},{64,128},{128,192},{192,256},{256,320},{320,384},{384,448},... | collective-permute-start | bytes 491528 | tf_op jit(solution)/shard_map/ppermute | solution.py:115
  95.3 27.7 %collective-permute-start.8 = (bf16[512,160]{0,1:T(8,128)(2,1)S(1)}, bf16[512,160]{0,1:T(8,128)(2,1)S(1)}, u32[]{:S(2)}, u32[]{:S(2)}) collective-permute-start(bf16[512,160]{0,1:T(8,128)(2,1)S(1)} %convolution_convert_fusion.5), channel_id=1, source_target_pairs={{0,128},{64,192},{128,256},{192,320},{256,384},{320,448},{384,0},{... | collective-permute-start | bytes 491528 | tf_op jit(solution)/shard_map/ppermute | solution.py:115
  98.6 27.7 %collective-permute-start.9 = (bf16[512,160]{0,1:T(8,128)(2,1)S(1)}, bf16[512,160]{0,1:T(8,128)(2,1)S(1)}, u32[]{:S(2)}, u32[]{:S(2)}) collective-permute-start(bf16[512,160]{0,1:T(8,128)(2,1)S(1)} %convolution_convert_fusion.4), channel_id=1, source_target_pairs={{0,192},{64,256},{128,320},{192,384},{256,448},{320,0},{384,64},{4... | collective-permute-start | bytes 491528 | tf_op jit(solution)/shard_map/ppermute | solution.py:115
  104.0 22.3 %collective-permute-start.10 = (bf16[512,160]{0,1:T(8,128)(2,1)S(1)}, bf16[512,160]{0,1:T(8,128)(2,1)S(1)}, u32[]{:S(2)}, u32[]{:S(2)}) collective-permute-start(bf16[512,160]{0,1:T(8,128)(2,1)S(1)} %convolution_convert_fusion.3), channel_id=1, source_target_pairs={{0,256},{64,320},{128,384},{192,448},{256,0},{320,64},{384,128},{4... | collective-permute-start | bytes 491528 | tf_op jit(solution)/shard_map/ppermute | solution.py:115
  111.1 17.8 %collective-permute-start.11 = (bf16[512,160]{0,1:T(8,128)(2,1)S(1)}, bf16[512,160]{0,1:T(8,128)(2,1)S(1)}, u32[]{:S(2)}, u32[]{:S(2)}) collective-permute-start(bf16[512,160]{0,1:T(8,128)(2,1)S(1)} %convolution_convert_fusion.2), channel_id=1, source_target_pairs={{0,320},{64,384},{128,448},{192,0},{256,64},{320,128},{384,192},{4... | collective-permute-start | bytes 491528 | tf_op jit(solution)/shard_map/ppermute | solution.py:115
  118.2 17.4 %collective-permute-start.12 = (bf16[512,160]{0,1:T(8,128)(2,1)S(1)}, bf16[512,160]{0,1:T(8,128)(2,1)S(1)}, u32[]{:S(2)}, u32[]{:S(2)}) collective-permute-start(bf16[512,160]{0,1:T(8,128)(2,1)S(1)} %convolution_convert_fusion.1), channel_id=1, source_target_pairs={{0,384},{64,448},{128,0},{192,64},{256,128},{320,192},{384,256},{4... | collective-permute-start | bytes 491528 | tf_op jit(solution)/shard_map/ppermute | solution.py:115
  123.0 14.3 %collective-permute-start.13 = (bf16[512,160]{0,1:T(8,128)(2,1)S(1)}, bf16[512,160]{0,1:T(8,128)(2,1)S(1)}, u32[]{:S(2)}, u32[]{:S(2)}) collective-permute-start(bf16[512,160]{0,1:T(8,128)(2,1)S(1)} %convolution_convert_fusion), channel_id=1, source_target_pairs={{0,448},{64,0},{128,64},{192,128},{256,192},{320,256},{384,320},{4... | collective-permute-start | bytes 491528 | tf_op jit(solution)/shard_map/ppermute | solution.py:115
